TPU v7x, 256 devices: a whole 4x4x8 slice. The times are simulated.
256 devices in a mesh: row: 32 (over z, y_hi, core), col: 8 (over x, y_lo).
Axes of the slice: x: 4, y: 4 (y_hi: 2, y_lo: 2; y = y_hi * 2 + y_lo), z: 8, core: 2. Of those that a mesh axis runs over, the one named last changes fastest.
Arguments:
- affinity_tiles: bfloat16 [1024, 512, 512], P(('row', 'col')), may hold values from -6 to 6
- tile_rows: int32 [1024], P(('row', 'col')), may hold values from -1 to 63, as said below
- tile_cols: int32 [1024], P(('row', 'col')), may hold values from -1 to 63, as said below
- lang_counts: int32 [32], replicated, may hold values from 1 to 8192, 32768 in all
- start_basis: float32 [8, 4096, 64], P('col', 'row'), may hold values from -6 to 6
Outputs:
- eigen_basis: float32 [8, 4096, 64], P('col', 'row')
Inputs may be any that keep to these rules, and one draw needn't show every extreme that they name: `tile_rows`: the slots of device (r, c) are entries (r * 8 + c) * 4 onward of both lists. Every used slot names a distinct block with block row from r * 2 to (r + 1) * 2 - 1, block column from c * 8 to (c + 1) * 8 - 1, and block row <= block column; no block is named twice. Empty slots hold -1 in both lists and come after the used slots of their device. Device (0, 7) uses all 4 slots. `tile_cols`: same slots as tile_rows.
All inputs are finite; a program needn't handle non-finite values.
Results may differ from a plain program's by a relative error of at most 0.0044.
Values may be sent and summed in bfloat16 or wider, within the bound.
No kernel may reach another device: no remote copies, remote signals or barrier semaphores. Data moves between devices by JAX's collectives and lax.ppermute only.
A program may use at most 64 MiB of HBM per device.

v0:
```python
import jax
import jax.numpy as jnp
from jax import lax
from jax.sharding import PartitionSpec as P

ROW_BLOCKS = 2
ITERS = 3
highest = lax.Precision.HIGHEST


def broadcast(value, axis, root):
    mine = lax.axis_index(axis) == root
    return lax.psum(jnp.where(mine, value, jnp.zeros_like(value)), axis)


def add_block(target, addend, offset):
    current = lax.dynamic_slice_in_dim(target, offset, addend.shape[0], 0)
    return lax.dynamic_update_slice_in_dim(target, current + addend, offset, 0)


def membership(first_doc, doc_count, lang_ends, lang_starts):
    doc_index = first_doc + jnp.arange(doc_count, dtype=jnp.int32)
    return (
        (doc_index[:, None] >= lang_starts[None, :]) & (doc_index[:, None] < lang_ends[None, :])
    ).astype(jnp.float32)


def apply_tiles(affinity_tiles, pick_rows, pick_cols, scaled_rows, scaled_cols, col_blocks):
    slot_count, tile_size, _ = affinity_tiles.shape
    vectors = scaled_cols.shape[1]
    blocks_r = scaled_rows.reshape(ROW_BLOCKS, tile_size, vectors)
    blocks_c = scaled_cols.reshape(col_blocks, tile_size, vectors)
    chosen_c = jnp.einsum(
        "tq,qjk->tjk", pick_cols, blocks_c, preferred_element_type=jnp.float32
    ).astype(jnp.bfloat16)
    chosen_r = jnp.einsum(
        "tp,pik->tik", pick_rows, blocks_r, preferred_element_type=jnp.float32
    ).astype(jnp.bfloat16)
    forward = jnp.einsum(
        "tij,tjk->tik", affinity_tiles, chosen_c, preferred_element_type=jnp.float32
    )
    backward = jnp.einsum(
        "tij,tik->tjk", affinity_tiles, chosen_r, preferred_element_type=jnp.float32
    )
    part_rows = jnp.einsum("tp,tik->pik", pick_rows.astype(jnp.float32), forward, precision=highest)
    part_cols = jnp.einsum(
        "tq,tjk->qjk", pick_cols.astype(jnp.float32), backward, precision=highest
    )
    return (
        part_rows.reshape(ROW_BLOCKS * tile_size, vectors),
        part_cols.reshape(col_blocks * tile_size, vectors),
    )


def shards(affinity_tiles, tile_rows, tile_cols, lang_counts, start_basis):
    row_devices = lax.axis_size("row")
    col_devices = lax.axis_size("col")
    group_ratio = row_devices // col_devices
    col_blocks = ROW_BLOCKS * row_devices // col_devices
    tile_size = affinity_tiles.shape[1]
    row_span = ROW_BLOCKS * tile_size
    col_span = col_blocks * tile_size
    piece_rows = start_basis.shape[1]
    doc_total = piece_rows * row_devices * col_devices
    my_row = lax.axis_index("row")
    my_col = lax.axis_index("col")
    is_owner = (my_row // group_ratio == my_col).astype(jnp.float32)
    offset = my_row % group_ratio * row_span
    piece_offset = my_row * piece_rows
    present = tile_rows >= 0
    local_p = tile_rows - my_row * ROW_BLOCKS
    local_q = tile_cols - my_col * col_blocks
    pick_rows = (
        (local_p[:, None] == jnp.arange(ROW_BLOCKS, dtype=jnp.int32)[None, :]) & present[:, None]
    ).astype(jnp.bfloat16)
    pick_cols = (
        (local_q[:, None] == jnp.arange(col_blocks, dtype=jnp.int32)[None, :]) & present[:, None]
    ).astype(jnp.bfloat16)
    magnitude = jnp.abs(affinity_tiles)
    row_mass = jnp.sum(magnitude, axis=2, dtype=jnp.float32)
    col_mass = jnp.sum(magnitude, axis=1, dtype=jnp.float32)
    degree_rows = jnp.einsum(
        "tp,ti->pi", pick_rows.astype(jnp.float32), row_mass, precision=highest
    ).reshape(row_span)
    degree_cols = jnp.einsum(
        "tq,tj->qj", pick_cols.astype(jnp.float32), col_mass, precision=highest
    ).reshape(col_span)
    rows_degree = lax.psum(degree_rows, "col")
    degree_cols = add_block(degree_cols, is_owner * rows_degree, offset)
    inv_own = lax.rsqrt(1.0 + lax.psum_scatter(degree_cols, "row", scatter_dimension=0, tiled=True))
    prior_scale = lax.psum(jnp.sum(inv_own), ("row", "col")) / doc_total
    lang_ends = jnp.cumsum(lang_counts)
    lang_starts = lang_ends - lang_counts
    counts_real = lang_counts.astype(jnp.float32)
    member_own = membership(my_col * col_span + piece_offset, piece_rows, lang_ends, lang_starts)
    basis_own = start_basis[0]
    for iteration in range(ITERS):
        lang_now = lax.psum(jnp.dot(member_own.T, basis_own, precision=highest), ("row", "col"))
        lang_mean = prior_scale * (lang_now / counts_real[:, None])
        scaled_cols = lax.all_gather(
            (inv_own[:, None] * basis_own).astype(jnp.bfloat16), "row", axis=0, tiled=True
        )
        scaled_rows = broadcast(
            lax.dynamic_slice_in_dim(scaled_cols, offset, row_span, 0), "col", my_row // group_ratio
        )
        part_rows, part_cols = apply_tiles(
            affinity_tiles, pick_rows, pick_cols, scaled_rows, scaled_cols, col_blocks
        )
        rows_sum = lax.psum(part_rows, "col")
        part_cols = add_block(part_cols, is_owner * rows_sum, offset)
        product_own = lax.psum_scatter(part_cols, "row", scatter_dimension=0, tiled=True)
        applied_own = inv_own[:, None] * product_own + jnp.dot(
            member_own, lang_mean, precision=highest
        )
        gram_part = jnp.dot(applied_own.T, applied_own, precision=highest)
        gram_matrix = lax.psum(gram_part, ("row", "col"))
        factor = jnp.linalg.cholesky(gram_matrix / doc_total)
        basis_own = jax.scipy.linalg.solve_triangular(factor, applied_own.T, lower=True).T
    return basis_own[None]


def solution(mesh):
    in_specs = (
        P(("row", "col"), None, None),
        P(("row", "col")),
        P(("row", "col")),
        P(),
        P("col", "row", None),
    )
    out_specs = P("col", "row", None)
    return jax.shard_map(shards, mesh=mesh, in_specs=in_specs, out_specs=out_specs, check_vma=False)
```

profile of v0, /device:TPU:1, one launch (start us, length us, event | category | flops | bytes accessed | tf_op | source)
XLA Modules:
  0.0 1385.8 jit_solution(9308302912916534671)
XLA Ops:
  8.6 2.2 convert_reduce_fusion
  11.0 16.9 %psum.98 = f32[1024]{0:T(1024)S(1)} all-reduce(f32[1024]{0:T(1024)S(1)} %bitcast.181), channel_id=1, replica_groups=mesh['row'=32,'col'=8] {'col'}, use_global_device_ids=true, to_apply=%region_2.3 | all-reduce | flops 1024 | bytes 8192 | tf_op jit(solution)/shard_map/psum | solution.py:88
  28.1 130.8 %all-reduce = f32[4096]{0:T(1024)S(1)} all-reduce(f32[4096]{0:T(1024)S(1)} %add_dynamic-update-slice_fusion.3), channel_id=2, replica_groups=mesh['row'=32,'col'=8] {'row'}, use_global_device_ids=true, to_apply=%region_3.4.clone | all-reduce | flops 4096 | bytes 32768
  160.8 43.6 %all_gather.9 = bf16[4096,64]{0,1:T(8,128)(2,1)S(1)} all-gather(bf16[128,64]{0,1:T(8,128)(2,1)S(1)} %fusion.39), channel_id=1, replica_groups=mesh['row'=32,'col'=8] {'row'}, dimensions={0}, use_global_device_ids=true | all-gather | bytes 540672 | tf_op jit(solution)/shard_map/all_gather | solution.py:100
  208.2 67.3 %all-reduce.9.cloned.1.call-done = bf16[2,512,64]{1,0,2:T(2,128)(2,1)} async-done(((bf16[2,512,64]{1,0,2:T(2,128)(2,1)}), bf16[2,512,64]{1,0,2:T(2,128)(2,1)}) %all-reduce.9.cloned.1.call-update) | async-done | bytes 131088 | tf_op jit(solution)/shard_map/psum | solution.py:13
  275.5 1.2 convolution_convert_fusion.5
  278.9 77.9 %all-reduce.11.cloned.1.call-done = f32[1024,64]{0,1:T(8,128)} async-done(((f32[1024,64]{0,1:T(8,128)}), f32[1024,64]{0,1:T(8,128)}) %all-reduce.11.cloned.1.call-update) | async-done | bytes 262160 | tf_op jit(solution)/shard_map/psum | solution.py:109
  359.3 79.9 %all-reduce.1 = (f32[32,64]{1,0:T(8,128)S(1)}, f32[]{:T(128)}) all-reduce(f32[32,64]{1,0:T(8,128)S(1)} %fusion.22, f32[]{:T(128)} %get-tuple-element.11), channel_id=1, replica_groups=mesh['row'=32,'col'=8] {'row','col'}, use_global_device_ids=true, to_apply=%region_10.11 | all-reduce | flops 2049 | bytes 16392 | tf_op jit(solution)/shard_map/psum | solution.py:98
  439.9 36.3 %reduce-scatter.4.cloned.1.call-done = f32[128,64]{0,1:T(8,128)} async-done(((f32[4096,64]{0,1:T(8,128)}), f32[128,64]{0,1:T(8,128)}) %reduce-scatter.4.cloned.1.call-update) | async-done | bytes 32784 | tf_op jit(solution)/shard_map/reduce_scatter | solution.py:111
  477.4 79.7 %psum.103 = f32[64,64]{0,1:T(8,128)S(1)} all-reduce(f32[64,64]{0,1:T(8,128)S(1)} %fusion.75), channel_id=1, replica_groups=mesh['row'=32,'col'=8] {'row','col'}, use_global_device_ids=true, to_apply=%region_11.12 | all-reduce | flops 4096 | bytes 32768 | tf_op jit(solution)/shard_map/psum | solution.py:116
  557.2 5.8 cholesky.59
  564.4 4.9 custom-call.7
  569.6 41.2 %all_gather.10 = bf16[4096,64]{0,1:T(8,128)(2,1)S(1)} all-gather(bf16[128,64]{0,1:T(8,128)(2,1)S(1)} %fusion.44), channel_id=1, replica_groups=mesh['row'=32,'col'=8] {'row'}, dimensions={0}, use_global_device_ids=true | all-gather | bytes 540672 | tf_op jit(solution)/shard_map/all_gather | solution.py:100
  614.7 65.5 %all-reduce.13.cloned.1.call-done = bf16[2,512,64]{1,0,2:T(2,128)(2,1)} async-done(((bf16[2,512,64]{1,0,2:T(2,128)(2,1)}), bf16[2,512,64]{1,0,2:T(2,128)(2,1)}) %all-reduce.13.cloned.1.call-update) | async-done | bytes 131088 | tf_op jit(solution)/shard_map/psum | solution.py:13
  680.2 1.2 convolution_convert_fusion.4
  683.5 77.7 %all-reduce.15.cloned.1.call-done = f32[1024,64]{0,1:T(8,128)} async-done(((f32[1024,64]{0,1:T(8,128)}), f32[1024,64]{0,1:T(8,128)}) %all-reduce.15.cloned.1.call-update) | async-done | bytes 262160 | tf_op jit(solution)/shard_map/psum | solution.py:109
  763.5 79.8 %psum.106 = f32[32,64]{1,0:T(8,128)S(1)} all-reduce(f32[32,64]{1,0:T(8,128)S(1)} %fusion.20), channel_id=1, replica_groups=mesh['row'=32,'col'=8] {'row','col'}, use_global_device_ids=true, to_apply=%region_17.20 | all-reduce | flops 2048 | bytes 16384 | tf_op jit(solution)/shard_map/psum | solution.py:98
  843.3 37.3 %reduce-scatter.6.cloned.1.call-done = f32[128,64]{0,1:T(8,128)} async-done(((f32[4096,64]{0,1:T(8,128)}), f32[128,64]{0,1:T(8,128)}) %reduce-scatter.6.cloned.1.call-update) | async-done | bytes 32784 | tf_op jit(solution)/shard_map/reduce_scatter | solution.py:111
  880.5 1.1 convolution_add_fusion.1
  881.8 79.7 %psum.107 = f32[64,64]{0,1:T(8,128)S(1)} all-reduce(f32[64,64]{0,1:T(8,128)S(1)} %fusion.76), channel_id=1, replica_groups=mesh['row'=32,'col'=8] {'row','col'}, use_global_device_ids=true, to_apply=%region_18.21 | all-reduce | flops 4096 | bytes 32768 | tf_op jit(solution)/shard_map/psum | solution.py:116
  961.6 5.8 cholesky.70
  968.8 4.9 custom-call.8
  974.0 41.2 %all_gather.11 = bf16[4096,64]{0,1:T(8,128)(2,1)S(1)} all-gather(bf16[128,64]{0,1:T(8,128)(2,1)S(1)} %fusion.45), channel_id=1, replica_groups=mesh['row'=32,'col'=8] {'row'}, dimensions={0}, use_global_device_ids=true | all-gather | bytes 540672 | tf_op jit(solution)/shard_map/all_gather | solution.py:100
  1019.1 65.4 %all-reduce.17.cloned.1.call-done = bf16[2,512,64]{1,0,2:T(2,128)(2,1)} async-done(((bf16[2,512,64]{1,0,2:T(2,128)(2,1)}), bf16[2,512,64]{1,0,2:T(2,128)(2,1)}) %all-reduce.17.cloned.1.call-update) | async-done | bytes 131088 | tf_op jit(solution)/shard_map/psum | solution.py:13
  1084.6 1.2 convolution_convert_fusion.3
  1087.9 77.9 %all-reduce.19.cloned.1.call-done = f32[1024,64]{0,1:T(8,128)} async-done(((f32[1024,64]{0,1:T(8,128)}), f32[1024,64]{0,1:T(8,128)}) %all-reduce.19.cloned.1.call-update) | async-done | bytes 262160 | tf_op jit(solution)/shard_map/psum | solution.py:109
  1168.0 79.8 %psum.110 = f32[32,64]{1,0:T(8,128)S(1)} all-reduce(f32[32,64]{1,0:T(8,128)S(1)} %fusion.18), channel_id=1, replica_groups=mesh['row'=32,'col'=8] {'row','col'}, use_global_device_ids=true, to_apply=%region_22.25 | all-reduce | flops 2048 | bytes 16384 | tf_op jit(solution)/shard_map/psum | solution.py:98
  1247.8 37.4 %reduce-scatter.8.cloned.1.call-done = f32[128,64]{0,1:T(8,128)} async-done(((f32[4096,64]{0,1:T(8,128)}), f32[128,64]{0,1:T(8,128)}) %reduce-scatter.8.cloned.1.call-update) | async-done | bytes 32784 | tf_op jit(solution)/shard_map/reduce_scatter | solution.py:111
  1285.2 1.1 convolution_add_fusion
  1286.5 79.7 %psum.111 = f32[64,64]{0,1:T(8,128)S(1)} all-reduce(f32[64,64]{0,1:T(8,128)S(1)} %fusion.77), channel_id=1, replica_groups=mesh['row'=32,'col'=8] {'row','col'}, use_global_device_ids=true, to_apply=%region_23.26 | all-reduce | flops 4096 | bytes 32768 | tf_op jit(solution)/shard_map/psum | solution.py:116
  1366.3 5.8 cholesky.81
  1373.5 4.9 custom-call.9
  (113 shorter events, 35.6 us)
Async XLA Ops:
  6.5 152.4 %copy-start.6 = (u32[256]{0:T(256)S(1)}, u32[256]{0:T(256)}, u32[]{:S(2)}) copy-start(u32[256]{0:T(256)} %constant.105) | copy-start | bytes 3076
  6.5 154.3 %copy-start.4 = (f32[1,128,64]{1,2,0:T(8,128)S(1)}, f32[1,128,64]{1,2,0:T(8,128)}, u32[]{:S(2)}) copy-start(f32[1,128,64]{1,2,0:T(8,128)} %param.12) | copy-start | bytes 98308
  6.5 269.0 %all-reduce.9.cloned.1.call-start = ((), (), s32[]{:S(2)}) async-start(), calls=%async_computation.3 | async-start | bytes 262144 | tf_op jit(solution)/shard_map/psum | solution.py:13
  10.8 194.9 %copy-start = (bf16[4,512,512]{2,1,0:T(8,128)(2,1)S(1)}, bf16[4,512,512]{2,1,0:T(8,128)(2,1)}, u32[]{:S(2)}) copy-start(bf16[4,512,512]{2,1,0:T(8,128)(2,1)} %param.8) | copy-start | bytes 6291460
  205.2 151.5 %all-reduce.11.cloned.1.call-start = ((), (), s32[]{:S(2)}) async-start(), calls=%async_computation.4 | async-start | bytes 524288 | tf_op jit(solution)/shard_map/psum | solution.py:109
  208.2 268.0 %reduce-scatter.4.cloned.1.call-start = ((), (), s32[]{:S(2)}) async-start(), calls=%async_computation.5 | async-start | bytes 1081344 | tf_op jit(solution)/shard_map/reduce_scatter | solution.py:111
  278.2 80.6 %copy-start.5 = (s32[32]{0:T(128)S(1)}, s32[32]{0:T(128)}, u32[]{:S(2)}) copy-start(s32[32]{0:T(128)} %param.11) | copy-start | bytes 388
  357.7 1.0 copy-start.2
  358.7 321.4 %all-reduce.13.cloned.1.call-start = ((), (), s32[]{:S(2)}) async-start(), calls=%async_computation.6 | async-start | bytes 262144 | tf_op jit(solution)/shard_map/psum | solution.py:13
  611.5 149.7 %all-reduce.15.cloned.1.call-start = ((), (), s32[]{:S(2)}) async-start(), calls=%async_computation.7 | async-start | bytes 524288 | tf_op jit(solution)/shard_map/psum | solution.py:109
  614.6 265.9 %reduce-scatter.6.cloned.1.call-start = ((), (), s32[]{:S(2)}) async-start(), calls=%async_computation.8 | async-start | bytes 1081344 | tf_op jit(solution)/shard_map/reduce_scatter | solution.py:111
  762.2 1.0 copy-start.3
  763.2 321.3 %all-reduce.17.cloned.1.call-start = ((), (), s32[]{:S(2)}) async-start(), calls=%async_computation.9 | async-start | bytes 262144 | tf_op jit(solution)/shard_map/psum | solution.py:13
  1015.9 149.9 %all-reduce.19.cloned.1.call-start = ((), (), s32[]{:S(2)}) async-start(), calls=%async_computation.10 | async-start | bytes 524288 | tf_op jit(solution)/shard_map/psum | solution.py:109
  1018.8 266.4 %reduce-scatter.8.cloned.1.call-start = ((), (), s32[]{:S(2)}) async-start(), calls=%async_computation.11 | async-start | bytes 1081344 | tf_op jit(solution)/shard_map/reduce_scatter | solution.py:111
  1166.8 1.0 copy-start.1
Sparse Core Ops, SparseCore 0:
  205.3 70.1 all-reduce.8
  278.1 78.5 all-reduce.10
  360.8 115.3 reduce-scatter.3
  611.6 68.4 all-reduce.12
  682.6 78.5 all-reduce.14
  765.1 115.3 reduce-scatter.5
  1016.0 68.5 all-reduce.16
  1087.2 78.5 all-reduce.18
  1169.8 115.3 reduce-scatter.7
where the time goes:
time: 1390 us
  blocking collectives  752 us (54%)
  waiting for transfers between devices  543 us (39%)
  other arithmetic  44.5 us (3%)
  matrix products  20 us (1%)
  between operations  15 us (1%)
    psum x3, blocking collectives, shards(): lax.psum(jnp.dot(member_own.T, basis_own, precision=highest), ('row', 'co...  239 us
    psum x3, blocking collectives, shards(): gram_matrix = lax.psum(gram_part, ('row', 'col'))  239 us
    psum x3, waiting for transfers between devices, shards(): rows_sum = lax.psum(part_rows, 'col')  233 us
    psum x3, waiting for transfers between devices, broadcast(): return lax.psum(jnp.where(mine, value, jnp.zeros_like(value)), axis)  198 us
    unnamed x1, blocking collectives  131 us
    all_gather x3, blocking collectives, shards(): lax.all_gather((inv_own[:, None] * basis_own).astype(jnp.bfloat16), 'row'...  126 us
    reduce_scatter x3, waiting for transfers between devices, shards(): lax.psum_scatter(part_cols, 'row', scatter_dimension=0, tiled=True)  111 us
  transfers between devices with their start and end apart: 9, of which 9 were waited for; matrix products, arithmetic and copies ran while one was open for 1% of the time, Pallas kernels for 0%

commit v1 on v0

--- a/solution.py
+++ b/solution.py
@@ -106,7 +106,7 @@
         part_rows, part_cols = apply_tiles(
             affinity_tiles, pick_rows, pick_cols, scaled_rows, scaled_cols, col_blocks
         )
-        rows_sum = lax.psum(part_rows, "col")
+        rows_sum = jnp.sum(lax.all_gather(part_rows, "col"), axis=0)
         part_cols = add_block(part_cols, is_owner * rows_sum, offset)
         product_own = lax.psum_scatter(part_cols, "row", scatter_dimension=0, tiled=True)
         applied_own = inv_own[:, None] * product_own + jnp.dot(

time: 1390 us -> 1310 us (0.942)
  waiting for transfers between devices: 543 us -> 468 us
    psum x3 -> x0, waiting for transfers between devices: 233 us -> none  [shards(): rows_sum = lax.psum(part_rows, 'col')]
    all_gather x0 -> x3, waiting for transfers between devices: none -> 165 us  [shards(): rows_sum = jnp.sum(lax.all_gather(part_rows, 'col'), axis=0)]
  transfers between devices with their start and end apart: 9 -> 9, of which waited for: 9 -> 9; matrix products, arithmetic and copies ran while one was open for 1% -> 2% of each run, Pallas kernels for 0% -> 0%
where the time goes in v1:
time: 1310 us
  blocking collectives  748 us (57%)
  waiting for transfers between devices  468 us (36%)
  other arithmetic  46.9 us (4%)
  matrix products  19.9 us (2%)
  between operations  15 us (1%)
    psum x3, blocking collectives, shards(): gram_matrix = lax.psum(gram_part, ('row', 'col'))  239 us
    psum x3, blocking collectives, shards(): lax.psum(jnp.dot(member_own.T, basis_own, precision=highest), ('row', 'co...  236 us
    psum x3, waiting for transfers between devices, broadcast(): return lax.psum(jnp.where(mine, value, jnp.zeros_like(value)), axis)  198 us
    all_gather x3, waiting for transfers between devices, shards(): rows_sum = jnp.sum(lax.all_gather(part_rows, 'col'), axis=0)  165 us
    unnamed x1, blocking collectives  131 us
    all_gather x3, blocking collectives, shards(): lax.all_gather((inv_own[:, None] * basis_own).astype(jnp.bfloat16), 'row'...  126 us
    reduce_scatter x3, waiting for transfers between devices, shards(): lax.psum_scatter(part_cols, 'row', scatter_dimension=0, tiled=True)  106 us
  transfers between devices with their start and end apart: 9, of which 9 were waited for; matrix products, arithmetic and copies ran while one was open for 2% of the time, Pallas kernels for 0%

profile of v1, /device:TPU:1, one launch (start us, length us, event | category | flops | bytes accessed | tf_op | source)
XLA Modules:
  0.0 1310.6 jit_solution(14737165555125877866)
XLA Ops:
  8.6 2.2 convert_reduce_fusion
  11.0 16.9 %psum.77 = f32[1024]{0:T(1024)S(1)} all-reduce(f32[1024]{0:T(1024)S(1)} %bitcast.169), channel_id=1, replica_groups=mesh['row'=32,'col'=8] {'col'}, use_global_device_ids=true, to_apply=%region_2.3 | all-reduce | flops 1024 | bytes 8192 | tf_op jit(solution)/shard_map/psum | solution.py:88
  28.1 130.8 %all-reduce = f32[4096]{0:T(1024)S(1)} all-reduce(f32[4096]{0:T(1024)S(1)} %add_dynamic-update-slice_fusion.3), channel_id=2, replica_groups=mesh['row'=32,'col'=8] {'row'}, use_global_device_ids=true, to_apply=%region_3.4.clone | all-reduce | flops 4096 | bytes 32768
  160.8 43.6 %all_gather.18 = bf16[4096,64]{0,1:T(8,128)(2,1)S(1)} all-gather(bf16[128,64]{0,1:T(8,128)(2,1)S(1)} %fusion.39), channel_id=1, replica_groups=mesh['row'=32,'col'=8] {'row'}, dimensions={0}, use_global_device_ids=true | all-gather | bytes 540672 | tf_op jit(solution)/shard_map/all_gather | solution.py:100
  208.4 67.1 %all-reduce.6.cloned.1.call-done = bf16[2,512,64]{1,0,2:T(2,128)(2,1)} async-done(((bf16[2,512,64]{1,0,2:T(2,128)(2,1)}), bf16[2,512,64]{1,0,2:T(2,128)(2,1)}) %all-reduce.6.cloned.1.call-update) | async-done | bytes 131088 | tf_op jit(solution)/shard_map/psum | solution.py:13
  275.5 1.2 convolution_convert_fusion.5
  278.9 54.9 %all-gather.4.cloned.1.call-done = f32[8,1024,64]{1,2,0:T(8,128)} async-done(((f32[1,1024,64]{1,2,0:T(8,128)}), f32[8,1024,64]{1,2,0:T(8,128)}) %all-gather.4.cloned.1.call-update) | async-done | bytes 2097168 | tf_op jit(solution)/shard_map/all_gather | solution.py:109
  333.8 1.8 reduce_sum.56
  337.2 78.7 %all-reduce.1 = (f32[32,64]{1,0:T(8,128)S(1)}, f32[]{:T(128)}) all-reduce(f32[32,64]{1,0:T(8,128)S(1)} %fusion.22, f32[]{:T(128)} %get-tuple-element.11), channel_id=1, replica_groups=mesh['row'=32,'col'=8] {'row','col'}, use_global_device_ids=true, to_apply=%region_10.11 | all-reduce | flops 2049 | bytes 16392 | tf_op jit(solution)/shard_map/psum | solution.py:98
  416.6 34.5 %reduce-scatter.4.cloned.1.call-done = f32[128,64]{0,1:T(8,128)} async-done(((f32[4096,64]{0,1:T(8,128)}), f32[128,64]{0,1:T(8,128)}) %reduce-scatter.4.cloned.1.call-update) | async-done | bytes 32784 | tf_op jit(solution)/shard_map/reduce_scatter | solution.py:111
  452.4 79.7 %psum.81 = f32[64,64]{0,1:T(8,128)S(1)} all-reduce(f32[64,64]{0,1:T(8,128)S(1)} %fusion.75), channel_id=1, replica_groups=mesh['row'=32,'col'=8] {'row','col'}, use_global_device_ids=true, to_apply=%region_11.12 | all-reduce | flops 4096 | bytes 32768 | tf_op jit(solution)/shard_map/psum | solution.py:116
  532.2 5.8 cholesky.59
  539.4 4.9 custom-call.7
  544.5 41.2 %all_gather.20 = bf16[4096,64]{0,1:T(8,128)(2,1)S(1)} all-gather(bf16[128,64]{0,1:T(8,128)(2,1)S(1)} %fusion.44), channel_id=1, replica_groups=mesh['row'=32,'col'=8] {'row'}, dimensions={0}, use_global_device_ids=true | all-gather | bytes 540672 | tf_op jit(solution)/shard_map/all_gather | solution.py:100
  589.9 65.3 %all-reduce.8.cloned.1.call-done = bf16[2,512,64]{1,0,2:T(2,128)(2,1)} async-done(((bf16[2,512,64]{1,0,2:T(2,128)(2,1)}), bf16[2,512,64]{1,0,2:T(2,128)(2,1)}) %all-reduce.8.cloned.1.call-update) | async-done | bytes 131088 | tf_op jit(solution)/shard_map/psum | solution.py:13
  658.4 54.8 %all-gather.6.cloned.1.call-done = f32[8,1024,64]{1,2,0:T(8,128)} async-done(((f32[1,1024,64]{1,2,0:T(8,128)}), f32[8,1024,64]{1,2,0:T(8,128)}) %all-gather.6.cloned.1.call-update) | async-done | bytes 2097168 | tf_op jit(solution)/shard_map/all_gather | solution.py:109
  713.2 1.8 reduce_sum.58
  716.4 78.6 %psum.83 = f32[32,64]{1,0:T(8,128)S(1)} all-reduce(f32[32,64]{1,0:T(8,128)S(1)} %fusion.20), channel_id=1, replica_groups=mesh['row'=32,'col'=8] {'row','col'}, use_global_device_ids=true, to_apply=%region_17.20 | all-reduce | flops 2048 | bytes 16384 | tf_op jit(solution)/shard_map/psum | solution.py:98
  794.9 35.5 %reduce-scatter.6.cloned.1.call-done = f32[128,64]{0,1:T(8,128)} async-done(((f32[4096,64]{0,1:T(8,128)}), f32[128,64]{0,1:T(8,128)}) %reduce-scatter.6.cloned.1.call-update) | async-done | bytes 32784 | tf_op jit(solution)/shard_map/reduce_scatter | solution.py:111
  831.7 79.7 %psum.84 = f32[64,64]{0,1:T(8,128)S(1)} all-reduce(f32[64,64]{0,1:T(8,128)S(1)} %fusion.76), channel_id=1, replica_groups=mesh['row'=32,'col'=8] {'row','col'}, use_global_device_ids=true, to_apply=%region_18.21 | all-reduce | flops 4096 | bytes 32768 | tf_op jit(solution)/shard_map/psum | solution.py:116
  911.5 5.8 cholesky.70
  918.7 4.9 custom-call.8
  923.9 41.2 %all_gather.22 = bf16[4096,64]{0,1:T(8,128)(2,1)S(1)} all-gather(bf16[128,64]{0,1:T(8,128)(2,1)S(1)} %fusion.45), channel_id=1, replica_groups=mesh['row'=32,'col'=8] {'row'}, dimensions={0}, use_global_device_ids=true | all-gather | bytes 540672 | tf_op jit(solution)/shard_map/all_gather | solution.py:100
  969.3 65.2 %all-reduce.10.cloned.1.call-done = bf16[2,512,64]{1,0,2:T(2,128)(2,1)} async-done(((bf16[2,512,64]{1,0,2:T(2,128)(2,1)}), bf16[2,512,64]{1,0,2:T(2,128)(2,1)}) %all-reduce.10.cloned.1.call-update) | async-done | bytes 131088 | tf_op jit(solution)/shard_map/psum | solution.py:13
  1034.5 1.2 convolution_convert_fusion.3
  1037.8 54.9 %all-gather.8.cloned.1.call-done = f32[8,1024,64]{1,2,0:T(8,128)} async-done(((f32[1,1024,64]{1,2,0:T(8,128)}), f32[8,1024,64]{1,2,0:T(8,128)}) %all-gather.8.cloned.1.call-update) | async-done | bytes 2097168 | tf_op jit(solution)/shard_map/all_gather | solution.py:109
  1092.7 1.8 reduce_sum.59
  1095.8 78.4 %psum.86 = f32[32,64]{1,0:T(8,128)S(1)} all-reduce(f32[32,64]{1,0:T(8,128)S(1)} %fusion.18), channel_id=1, replica_groups=mesh['row'=32,'col'=8] {'row','col'}, use_global_device_ids=true, to_apply=%region_22.25 | all-reduce | flops 2048 | bytes 16384 | tf_op jit(solution)/shard_map/psum | solution.py:98
  1174.2 35.8 %reduce-scatter.8.cloned.1.call-done = f32[128,64]{0,1:T(8,128)} async-done(((f32[4096,64]{0,1:T(8,128)}), f32[128,64]{0,1:T(8,128)}) %reduce-scatter.8.cloned.1.call-update) | async-done | bytes 32784 | tf_op jit(solution)/shard_map/reduce_scatter | solution.py:111
  1211.3 79.7 %psum.87 = f32[64,64]{0,1:T(8,128)S(1)} all-reduce(f32[64,64]{0,1:T(8,128)S(1)} %fusion.77), channel_id=1, replica_groups=mesh['row'=32,'col'=8] {'row','col'}, use_global_device_ids=true, to_apply=%region_23.26 | all-reduce | flops 4096 | bytes 32768 | tf_op jit(solution)/shard_map/psum | solution.py:116
  1291.1 5.8 cholesky.81
  1298.3 4.9 custom-call.9
  (116 shorter events, 36.8 us)
Async XLA Ops:
  6.5 152.4 %copy-start.6 = (u32[256]{0:T(256)S(1)}, u32[256]{0:T(256)}, u32[]{:S(2)}) copy-start(u32[256]{0:T(256)} %constant.105) | copy-start | bytes 3076
  6.5 154.3 %copy-start.4 = (f32[1,128,64]{1,2,0:T(8,128)S(1)}, f32[1,128,64]{1,2,0:T(8,128)}, u32[]{:S(2)}) copy-start(f32[1,128,64]{1,2,0:T(8,128)} %param.12) | copy-start | bytes 98308
  6.5 269.0 %all-reduce.6.cloned.1.call-start = ((), (), s32[]{:S(2)}) async-start(), calls=%async_computation.3 | async-start | bytes 262144 | tf_op jit(solution)/shard_map/psum | solution.py:13
  10.8 194.9 %copy-start = (bf16[4,512,512]{2,1,0:T(8,128)(2,1)S(1)}, bf16[4,512,512]{2,1,0:T(8,128)(2,1)}, u32[]{:S(2)}) copy-start(bf16[4,512,512]{2,1,0:T(8,128)(2,1)} %param.8) | copy-start | bytes 6291460
  205.2 128.6 %all-gather.4.cloned.1.call-start = ((), (), s32[]{:S(2)}) async-start(), calls=%async_computation.4 | async-start | bytes 2359296 | tf_op jit(solution)/shard_map/all_gather | solution.py:109
  208.4 242.7 %reduce-scatter.4.cloned.1.call-start = ((), (), s32[]{:S(2)}) async-start(), calls=%async_computation.5 | async-start | bytes 1081344 | tf_op jit(solution)/shard_map/reduce_scatter | solution.py:111
  278.9 57.8 %copy-start.5 = (s32[32]{0:T(128)S(1)}, s32[32]{0:T(128)}, u32[]{:S(2)}) copy-start(s32[32]{0:T(128)} %param.11) | copy-start | bytes 388
  335.6 1.0 copy-start.2
  336.6 318.5 %all-reduce.8.cloned.1.call-start = ((), (), s32[]{:S(2)}) async-start(), calls=%async_computation.6 | async-start | bytes 262144 | tf_op jit(solution)/shard_map/psum | solution.py:13
  586.5 126.7 %all-gather.6.cloned.1.call-start = ((), (), s32[]{:S(2)}) async-start(), calls=%async_computation.7 | async-start | bytes 2359296 | tf_op jit(solution)/shard_map/all_gather | solution.py:109
  589.8 240.6 %reduce-scatter.6.cloned.1.call-start = ((), (), s32[]{:S(2)}) async-start(), calls=%async_computation.8 | async-start | bytes 1081344 | tf_op jit(solution)/shard_map/reduce_scatter | solution.py:111
  715.1 1.0 copy-start.3
  716.1 318.4 %all-reduce.10.cloned.1.call-start = ((), (), s32[]{:S(2)}) async-start(), calls=%async_computation.9 | async-start | bytes 262144 | tf_op jit(solution)/shard_map/psum | solution.py:13
  965.8 126.9 %all-gather.8.cloned.1.call-start = ((), (), s32[]{:S(2)}) async-start(), calls=%async_computation.10 | async-start | bytes 2359296 | tf_op jit(solution)/shard_map/all_gather | solution.py:109
  969.0 241.1 %reduce-scatter.8.cloned.1.call-start = ((), (), s32[]{:S(2)}) async-start(), calls=%async_computation.11 | async-start | bytes 1081344 | tf_op jit(solution)/shard_map/reduce_scatter | solution.py:111
  1094.5 1.0 copy-start.1
Sparse Core Ops, SparseCore 0:
  205.3 70.1 all-reduce.5
  277.3 56.4 all-gather.3
  337.9 113.1 reduce-scatter.3
  586.6 68.4 all-reduce.7
  656.8 56.4 all-gather.5
  717.2 113.2 reduce-scatter.5
  966.0 68.4 all-reduce.9
  1036.3 56.4 all-gather.7
  1096.8 113.1 reduce-scatter.7
